TPU v7x, 512 devices: a whole 4x4x16 slice. The times are simulated.
512 devices in a mesh: section: 2 (over core), expert: 32 (over z_lo, x), tensor: 8 (over y, z_hi).
Axes of the slice: x: 4, y: 4, z: 16 (z_hi: 2, z_lo: 8; z = z_hi * 8 + z_lo), core: 2. Of those that a mesh axis runs over, the one named last changes fastest.
Arguments:
- sent: bfloat16 [2, 4096, 4096], P('section', ('expert', 'tensor')), may hold values from -20 to 20
- norm_gain: float32 [2, 4096], P('section'), may hold values from 0.1 to 1.9
- router: bfloat16 [2, 4096, 32], P('section'), may hold values from -0.09375 to 0.09375
- w_in: bfloat16 [2, 32, 4096, 2048], P('section', 'expert', None, 'tensor'), may hold values from -0.09375 to 0.09375
- w_out: bfloat16 [2, 32, 2048, 4096], P('section', 'expert', 'tensor'), may hold values from -0.125 to 0.125
- expert_ids: int32 [2, 4096, 2], P('section', ('expert', 'tensor')), may hold values from 0 to 31, as said below
Outputs:
- handed: bfloat16 [2, 4096, 4096], P('section', ('expert', 'tensor'))
Inputs may be any that keep to these rules, and one draw needn't show every extreme that they name: `expert_ids`: each token names two different experts of the 32.
All inputs are finite; a program needn't handle non-finite values.
Results may differ from a plain program's by a relative error of at most 0.0054.
Values may be sent and summed in bfloat16 or wider, within the bound.
No kernel may reach another device: no remote copies, remote signals or barrier semaphores. Data moves between devices by JAX's collectives and lax.ppermute only.
A program may use at most 64 MiB of HBM per device.

v0:
```python
import jax
import jax.numpy as jnp
from jax import lax
from jax.sharding import Mesh
from jax.sharding import PartitionSpec as P


def passed_along(value, axis, steps):
    count = lax.axis_size(axis)
    pairs = [(source, (source + steps) % count) for source in range(count)]
    return lax.ppermute(value, axis, pairs)


def normalize(inputs, gain_row):
    widened = inputs.astype(jnp.float32)
    mean_sq = jnp.mean(widened * widened, axis=-1, keepdims=True)
    return (widened * lax.rsqrt(mean_sq + 1e-05) * gain_row).astype(jnp.bfloat16)


def route(normed, router_mat, expert_pick, tok_block, capacity):
    logits = jnp.dot(normed, router_mat, preferred_element_type=jnp.float32)
    experts = router_mat.shape[1]
    labels = jnp.arange(experts, dtype=jnp.int32)
    pair_hot = (expert_pick[:, :, None] == labels[None, None, :]).astype(jnp.float32)
    picked = jnp.sum(pair_hot * logits[:, None, :], axis=-1)
    squashed = jax.nn.sigmoid(picked)
    gate_vals = squashed / jnp.sum(squashed, axis=-1, keepdims=True)
    blocks = expert_pick.shape[0] // tok_block
    pair_order = jnp.transpose(expert_pick.reshape(blocks, tok_block, 2), (0, 2, 1)).reshape(
        blocks, 2 * tok_block
    )
    one_hot = (pair_order[:, :, None] == labels[None, None, :]).astype(jnp.int32)
    before = jnp.cumsum(one_hot, axis=1) - one_hot
    pair_ranks = jnp.sum(before * one_hot, axis=-1)
    pair_ranks = jnp.transpose(pair_ranks.reshape(blocks, 2, tok_block), (0, 2, 1)).reshape(-1, 2)
    is_kept = pair_ranks < capacity
    return (gate_vals, pair_ranks, is_kept)


def on_device(sent, norm_gain, router, w_in, w_out, expert_ids):
    arrived = passed_along(sent, "section", 1)[0]
    tok_count = arrived.shape[0]
    model_width = arrived.shape[1]
    experts = router.shape[2]
    top_count = expert_ids.shape[2]
    n_y = lax.axis_size("y")
    capacity = max(2, (5 * top_count * tok_count + 4 * experts - 1) // (4 * experts))
    normed = normalize(arrived, norm_gain[0])
    own_pick = expert_ids[0]
    partner_rows = passed_along(normed, "zh", 1)
    partner_pick = passed_along(own_pick, "zh", 1)
    rows_both = jnp.concatenate([normed, partner_rows], axis=0)
    pick_both = jnp.concatenate([own_pick, partner_pick], axis=0)
    gate_vals, pair_ranks, is_kept = route(rows_both, router[0], pick_both, tok_count, capacity)
    n_tok = 2 * tok_count
    block_of = (jnp.arange(n_tok, dtype=jnp.int32) // tok_count)[:, None]
    per_expert = 2 * capacity
    slot_ids = pick_both * per_expert + block_of * capacity + pair_ranks
    slot_count = experts * per_expert
    slot_labels = jnp.arange(slot_count, dtype=jnp.int32)
    slot_hot = ((slot_ids[:, :, None] == slot_labels[None, None, :]) & is_kept[:, :, None]).astype(
        jnp.float32
    )
    placement = jnp.transpose(jnp.sum(slot_hot, axis=1)).astype(jnp.bfloat16)
    combine_mat = jnp.sum(slot_hot * gate_vals[:, :, None], axis=1)
    send_rows = jnp.dot(placement, rows_both, preferred_element_type=jnp.float32).astype(
        jnp.bfloat16
    )
    slot_grid = send_rows.reshape(experts, per_expert, model_width)
    received = lax.all_to_all(slot_grid, "expert", split_axis=0, concat_axis=0, tiled=True)
    gathered = lax.all_gather(received[None], "y", axis=0, tiled=True)
    rows_in = gathered.reshape(-1, model_width)
    hidden = jax.nn.gelu(jnp.dot(rows_in, w_in[0, 0], preferred_element_type=jnp.float32)).astype(
        jnp.bfloat16
    )
    partial = jnp.dot(hidden, w_out[0, 0], preferred_element_type=jnp.float32).astype(jnp.bfloat16)
    summed = lax.psum_scatter(
        partial.reshape(n_y, -1, model_width), "y", scatter_dimension=0, tiled=True
    )
    back = lax.all_to_all(
        summed.reshape(experts, per_expert, model_width),
        "expert",
        split_axis=0,
        concat_axis=0,
        tiled=True,
    )
    half_sum = jnp.dot(
        combine_mat,
        back.reshape(slot_count, model_width).astype(jnp.float32),
        precision=lax.Precision.HIGHEST,
    )
    from_partner = passed_along(half_sum[tok_count:].astype(jnp.bfloat16), "zh", 1)
    combined = arrived.astype(jnp.float32) + half_sum[:tok_count] + from_partner.astype(jnp.float32)
    return passed_along(combined.astype(jnp.bfloat16)[None], "section", 1)


def solution(mesh):
    sizes = dict(mesh.shape)
    n_tensor = sizes["tensor"]
    fine = Mesh(
        mesh.devices.reshape(sizes["section"], sizes["expert"], n_tensor // 2, 2),
        ("section", "expert", "y", "zh"),
    )
    tokens = ("expert", "y", "zh")
    hidden_units = ("y", "zh")
    return jax.shard_map(
        on_device,
        mesh=fine,
        in_specs=(
            P("section", tokens, None),
            P("section", None),
            P("section", None, None),
            P("section", "expert", None, hidden_units),
            P("section", "expert", hidden_units, None),
            P("section", tokens, None),
        ),
        out_specs=P("section", tokens, None),
        check_vma=False,
    )
```

profile of v0, /device:TPU:3, one launch (start us, length us, event | category | flops | bytes accessed | tf_op | source)
XLA Modules:
  0.0 338.4 jit_solution(3203111217646648346)
XLA Ops:
  6.5 0.0 copy-start
  6.5 0.0 all-gather.3.cloned.1.call-start
  6.5 15.6 %collective-permute-start.1 = (s32[16,2]{0,1:T(2,128)}, s32[16,2]{0,1:T(2,128)S(1)}, u32[]{:S(2)}, u32[]{:S(2)}) collective-permute-start(s32[16,2]{0,1:T(2,128)} %bitcast.39), channel_id=1, source_target_pairs={{0,1},{1,0},{2,3},{3,2},{4,5},{5,4},{6,7},{7,6},{8,9},{9,8},{10,11... | collective-permute-start | bytes 392 | tf_op jit(solution)/shard_map/ppermute | solution.py:11
  22.1 2.9 collective-permute-start
  25.0 0.0 collective-permute-done.1
  25.0 0.8 pad_add_fusion
  25.8 0.1 reshape.115
  25.9 0.1 eq.20
  25.9 0.1 fusion.29
  26.0 0.1 reduce_window_sum.11
  26.1 0.2 select_reduce_fusion.2
  26.3 0.1 reshape.116
  26.3 0.1 reshape.117
  26.4 0.8 add_add_fusion
  27.2 0.0 collective-permute-done
  27.2 0.1 fusion.17
  27.4 0.8 fusion.19
  28.2 10.3 %collective-permute-start.2 = (bf16[16,4096]{1,0:T(8,128)(2,1)S(1)}, bf16[16,4096]{1,0:T(8,128)(2,1)S(1)}, u32[]{:S(2)}, u32[]{:S(2)}) collective-permute-start(bf16[16,4096]{1,0:T(8,128)(2,1)S(1)} %fusion.19), channel_id=1, source_target_pairs={{0,1},{1,0},{2,3},{3,2},{4,5},{5,4},{6,7},{7,6},{8,9},{9,8},{10,11... | collective-permute-start | bytes 393224 | tf_op jit(solution)/shard_map/ppermute | solution.py:11
  38.5 5.3 %collective-permute-done.2 = bf16[16,4096]{1,0:T(8,128)(2,1)S(1)} collective-permute-done((bf16[16,4096]{1,0:T(8,128)(2,1)S(1)}, bf16[16,4096]{1,0:T(8,128)(2,1)S(1)}, u32[]{:S(2)}, u32[]{:S(2)}) %collective-permute-start.2) | collective-permute-done | bytes 131104 | tf_op jit(solution)/shard_map/ppermute | solution.py:11
  43.8 1.1 fusion.22
  45.0 0.2 select_reduce_fusion.1
  45.2 0.1 convert_reduce_fusion
  45.3 0.5 convolution_convert_fusion.1
  45.8 1.2 reshape.118
  47.0 65.4 %all_to_all.10 = bf16[32,4,4096]{2,1,0:T(4,128)(2,1)} all-to-all(bf16[32,4,4096]{2,1,0:T(4,128)(2,1)} %reshape.118), channel_id=1, replica_groups=mesh['section'=2,'expert'=32,'y'=4,'zh'=2] {'expert'}, dimensions={0} | all-to-all | bytes 2097152 | tf_op jit(solution)/shard_map/all_to_all | solution.py:70
  112.4 0.0 all-gather.3.cloned.1.call-update
  112.4 0.0 reduce-scatter.2.cloned.1.call-start
  112.5 56.1 %all-gather.3.cloned.1.call-done = bf16[128,4,4096]{2,1,0:T(4,128)(2,1)} async-done(((bf16[32,4,4096]{2,1,0:T(4,128)(2,1)}), bf16[128,4,4096]{2,1,0:T(4,128)(2,1)}) %all-gather.3.cloned.1.call-update) | async-done | bytes 4194320 | tf_op jit(solution)/shard_map/all_gather | solution.py:71
  168.6 6.9 %reshape.119 = bf16[512,4096]{1,0:T(8,128)(2,1)} reshape(bf16[128,4,4096]{2,1,0:T(4,128)(2,1)} %all-gather.3.cloned.1.call-done) | data formatting | bytes 8388608 | tf_op jit(solution)/shard_map/reshape | solution.py:72
  175.5 0.0 copy-done
  175.5 9.3 %convolution_convert_fusion = bf16[512,4096]{1,0:T(8,128)(2,1)} fusion(bf16[1,1,256,4096]{3,2,1,0:T(8,128)(2,1)S(1)} %copy-done, bf16[512,4096]{1,0:T(8,128)(2,1)} %reshape.119, bf16[1,1,4096,256]{3,2,1,0:T(8,128)(2,1)} %param.9), kind=kOutput, calls=%fused_computation | convolution fusion | flops 2150760448 | bytes 12582912 | tf_op jit(solution)/shard_map/dot_general | solution.py:76
  184.8 0.0 reduce-scatter.2.cloned.1.call-update
  184.8 55.2 %reduce-scatter.2.cloned.1.call-done = bf16[1,128,4096]{2,1,0:T(8,128)(2,1)} async-done(((bf16[4,128,4096]{2,1,0:T(8,128)(2,1)}), bf16[1,128,4096]{2,1,0:T(8,128)(2,1)}) %reduce-scatter.2.cloned.1.call-update) | async-done | bytes 1048592 | tf_op jit(solution)/shard_map/reduce_scatter | solution.py:77
  240.0 1.5 reshape.121
  241.5 62.2 %all_to_all.11 = bf16[32,4,4096]{2,1,0:T(4,128)(2,1)} all-to-all(bf16[32,4,4096]{2,1,0:T(4,128)(2,1)S(1)} %reshape.121), channel_id=1, replica_groups=mesh['section'=2,'expert'=32,'y'=4,'zh'=2] {'expert'}, dimensions={0} | all-to-all | bytes 2097152 | tf_op jit(solution)/shard_map/all_to_all | solution.py:80
  303.7 1.3 reshape.122
  305.0 0.5 fusion.39
  305.6 5.0 %collective-permute-start.3 = (bf16[16,4096]{1,0:T(8,128)(2,1)S(1)}, bf16[16,4096]{1,0:T(8,128)(2,1)S(1)}, u32[]{:S(2)}, u32[]{:S(2)}) collective-permute-start(bf16[16,4096]{1,0:T(8,128)(2,1)S(1)} %slice.15), channel_id=1, source_target_pairs={{0,1},{1,0},{2,3},{3,2},{4,5},{5,4},{6,7},{7,6},{8,9},{9,8},{10,11... | collective-permute-start | bytes 393224 | tf_op jit(solution)/shard_map/ppermute | solution.py:11
  310.6 16.9 %collective-permute-done.3 = bf16[16,4096]{1,0:T(8,128)(2,1)S(1)} collective-permute-done((bf16[16,4096]{1,0:T(8,128)(2,1)S(1)}, bf16[16,4096]{1,0:T(8,128)(2,1)S(1)}, u32[]{:S(2)}, u32[]{:S(2)}) %collective-permute-start.3) | collective-permute-done | bytes 131104 | tf_op jit(solution)/shard_map/ppermute | solution.py:11
  327.5 0.1 fusion.28
  327.5 2.4 collective-permute-start.4
  330.0 1.0 collective-permute-done.4
  331.0 0.7 copy.20
  (8 shorter events, 0.1 us)
Async XLA Ops:
  6.5 169.0 %copy-start = (bf16[1,1,256,4096]{3,2,1,0:T(8,128)(2,1)S(1)}, bf16[1,1,256,4096]{3,2,1,0:T(8,128)(2,1)}, u32[]{:S(2)}) copy-start(bf16[1,1,256,4096]{3,2,1,0:T(8,128)(2,1)} %param.10) | copy-start | bytes 6291460
  6.5 162.0 %all-gather.3.cloned.1.call-start = ((), (), s32[]{:S(2)}) async-start(), calls=%async_computation.4 | async-start | bytes 5242880 | tf_op jit(solution)/shard_map/all_gather | solution.py:71
  6.5 18.5 %collective-permute-start.1 = (s32[16,2]{0,1:T(2,128)}, s32[16,2]{0,1:T(2,128)S(1)}, u32[]{:S(2)}, u32[]{:S(2)}) collective-permute-start(s32[16,2]{0,1:T(2,128)} %bitcast.39), channel_id=1, source_target_pairs={{0,1},{1,0},{2,3},{3,2},{4,5},{5,4},{6,7},{7,6},{8,9},{9,8},{10,11... | collective-permute-start | bytes 392 | tf_op jit(solution)/shard_map/ppermute | solution.py:11
  22.1 5.1 %collective-permute-start = (bf16[1,16,4096]{2,1,0:T(8,128)(2,1)}, bf16[1,16,4096]{2,1,0:T(8,128)(2,1)S(1)}, u32[]{:S(2)}, u32[]{:S(2)}) collective-permute-start(bf16[1,16,4096]{2,1,0:T(8,128)(2,1)} %param.6), channel_id=1, source_target_pairs={{0,256},{256,0},{1,257},{257,1},{2,258},{258,2},{3,259},{259,3},{4... | collective-permute-start | bytes 393224 | tf_op jit(solution)/shard_map/ppermute | solution.py:11
  28.2 15.7 %collective-permute-start.2 = (bf16[16,4096]{1,0:T(8,128)(2,1)S(1)}, bf16[16,4096]{1,0:T(8,128)(2,1)S(1)}, u32[]{:S(2)}, u32[]{:S(2)}) collective-permute-start(bf16[16,4096]{1,0:T(8,128)(2,1)S(1)} %fusion.19), channel_id=1, source_target_pairs={{0,1},{1,0},{2,3},{3,2},{4,5},{5,4},{6,7},{7,6},{8,9},{9,8},{10,11... | collective-permute-start | bytes 393224 | tf_op jit(solution)/shard_map/ppermute | solution.py:11
  112.4 127.6 %reduce-scatter.2.cloned.1.call-start = ((), (), s32[]{:S(2)}) async-start(), calls=%async_computation.3 | async-start | bytes 5242880 | tf_op jit(solution)/shard_map/reduce_scatter | solution.py:77
  305.6 21.9 %collective-permute-start.3 = (bf16[16,4096]{1,0:T(8,128)(2,1)S(1)}, bf16[16,4096]{1,0:T(8,128)(2,1)S(1)}, u32[]{:S(2)}, u32[]{:S(2)}) collective-permute-start(bf16[16,4096]{1,0:T(8,128)(2,1)S(1)} %slice.15), channel_id=1, source_target_pairs={{0,1},{1,0},{2,3},{3,2},{4,5},{5,4},{6,7},{7,6},{8,9},{9,8},{10,11... | collective-permute-start | bytes 393224 | tf_op jit(solution)/shard_map/ppermute | solution.py:11
  327.5 3.4 %collective-permute-start.4 = (bf16[1,16,4096]{2,1,0:T(8,128)(2,1)S(1)}, bf16[1,16,4096]{2,1,0:T(8,128)(2,1)S(1)}, u32[]{:S(2)}, u32[]{:S(2)}) collective-permute-start(bf16[1,16,4096]{2,1,0:T(8,128)(2,1)S(1)} %fusion.28), channel_id=1, source_target_pairs={{0,256},{256,0},{1,257},{257,1},{2,258},{258,2},{3,259},{259,3},{4... | collective-permute-start | bytes 393224 | tf_op jit(solution)/shard_map/ppermute | solution.py:11
Sparse Core Ops, SparseCore 0:
  112.6 55.9 all-gather.2
  184.9 55.0 reduce-scatter.1
where the time goes:
time: 339 us; the launch traced here: 338 us
  waiting for transfers between devices  134 us (40%)
  blocking collectives  128 us (38%)
  starting transfers between devices  36.3 us (11%)
  between operations  13.5 us (4%)
  local copies, waits for them, and re-layouts  11.9 us (4%)
  matrix products  11.4 us (3%)
    all_to_all x1, blocking collectives, on_device(): lax.all_to_all(slot_grid, 'expert', split_axis=0, concat_axis=0, tiled=True)  65.4 us
    all_to_all x1, blocking collectives, on_device(): lax.all_to_all(summed.reshape(experts, per_expert, model_width), 'expert'...  62.2 us
    all_gather x1, waiting for transfers between devices, on_device(): gathered = lax.all_gather(received[None], 'y', axis=0, tiled=True)  56.1 us
    reduce_scatter x1, waiting for transfers between devices, on_device(): lax.psum_scatter(partial.reshape(n_y, -1, model_width), 'y', scatter_dime...  55.2 us
    ppermute x5, starting transfers between devices, passed_along(): return lax.ppermute(value, axis, pairs)  36.2 us
    ppermute x5, waiting for transfers between devices, passed_along(): return lax.ppermute(value, axis, pairs)  23.1 us
    dot_general x1, matrix products, on_device(): jnp.dot(hidden, w_out[0, 0], preferred_element_type=jnp.float32)  9.31 us
    reshape x1, local copies, waits for them, and re-layouts, on_device(): rows_in = gathered.reshape(-1, model_width)  6.91 us
  transfers between devices with their start and end apart: 7, of which 5 were waited for; matrix products, arithmetic and copies ran while one was open for 1% of the time, Pallas kernels for 0%

commit v1 on v0

--- a/solution.py
+++ b/solution.py
@@ -68,7 +68,9 @@
     )
     slot_grid = send_rows.reshape(experts, per_expert, model_width)
     received = lax.all_to_all(slot_grid, "expert", split_axis=0, concat_axis=0, tiled=True)
-    gathered = lax.all_gather(received[None], "y", axis=0, tiled=True)
+    gathered = jnp.concatenate(
+        lax.all_to_all(jnp.stack([received[None]] * lax.axis_size("y")), "y", 0, 0), axis=0
+    )
     rows_in = gathered.reshape(-1, model_width)
     hidden = jax.nn.gelu(jnp.dot(rows_in, w_in[0, 0], preferred_element_type=jnp.float32)).astype(
         jnp.bfloat16

time: 339 us -> 335 us (0.988)
  waiting for transfers between devices: 134 us -> 77.8 us
  blocking collectives: 128 us -> 178 us
    all_gather x1 -> x0, waiting for transfers between devices: 56.1 us -> none  [on_device(): gathered = lax.all_gather(received[None], 'y', axis=0, tiled=True)]
    all_to_all x0 -> x1, blocking collectives: none -> 50.4 us  [on_device(): lax.all_to_all(jnp.stack([received[None]] * lax.axis_size('y')), 'y', 0, 0)]
    another operation x0 -> x2, local copies, waits for them, and re-layouts: none -> 9.01 us  [the longest x1 6.92 us: on_device(): rows_in = gathered.reshape(-1, model_width)]
    reshape x1 -> x0, local copies, waits for them, and re-layouts: 6.91 us -> none  [on_device(): rows_in = gathered.reshape(-1, model_width)]
  transfers between devices with their start and end apart: 7 -> 6, of which waited for: 5 -> 4; matrix products, arithmetic and copies ran while one was open for 1% -> 1% of each run, Pallas kernels for 0% -> 0%
where the time goes in v1:
time: 335 us; the launch traced here: 334 us
  blocking collectives  178 us (53%)
  waiting for transfers between devices  77.8 us (23%)
  starting transfers between devices  36.2 us (11%)
  local copies, waits for them, and re-layouts  14 us (4%)
  between operations  13.5 us (4%)
  matrix products  11.5 us (3%)
    all_to_all x1, blocking collectives, on_device(): lax.all_to_all(slot_grid, 'expert', split_axis=0, concat_axis=0, tiled=True)  65.3 us
    all_to_all x1, blocking collectives, on_device(): lax.all_to_all(summed.reshape(experts, per_expert, model_width), 'expert'...  62.2 us
    reduce_scatter x1, waiting for transfers between devices, on_device(): lax.psum_scatter(partial.reshape(n_y, -1, model_width), 'y', scatter_dime...  54.6 us
    all_to_all x1, blocking collectives, on_device(): lax.all_to_all(jnp.stack([received[None]] * lax.axis_size('y')), 'y', 0, 0)  50.4 us
    ppermute x5, starting transfers between devices, passed_along(): return lax.ppermute(value, axis, pairs)  36.2 us
    ppermute x5, waiting for transfers between devices, passed_along(): return lax.ppermute(value, axis, pairs)  23.1 us
    dot_general x1, matrix products, on_device(): jnp.dot(hidden, w_out[0, 0], preferred_element_type=jnp.float32)  9.35 us
    another operation x1, local copies, waits for them, and re-layouts, on_device(): rows_in = gathered.reshape(-1, model_width)  6.92 us
  transfers between devices with their start and end apart: 6, of which 4 were waited for; matrix products, arithmetic and copies ran while one was open for 1% of the time, Pallas kernels for 0%

profile of v1, /device:TPU:3, one launch (start us, length us, event | category | flops | bytes accessed | tf_op | source)
XLA Modules:
  0.0 334.1 jit_solution(5333682980645637386)
XLA Ops:
  6.5 0.0 copy-start
  6.5 0.0 reduce-scatter.2.cloned.1.call-start
  6.5 15.6 %collective-permute-start.1 = (s32[16,2]{0,1:T(2,128)}, s32[16,2]{0,1:T(2,128)S(1)}, u32[]{:S(2)}, u32[]{:S(2)}) collective-permute-start(s32[16,2]{0,1:T(2,128)} %bitcast.39), channel_id=1, source_target_pairs={{0,1},{1,0},{2,3},{3,2},{4,5},{5,4},{6,7},{7,6},{8,9},{9,8},{10,11... | collective-permute-start | bytes 392 | tf_op jit(solution)/shard_map/ppermute | solution.py:11
  22.1 2.9 collective-permute-start
  25.0 0.0 collective-permute-done.1
  25.0 0.8 pad_add_fusion
  25.8 0.1 reshape.114
  25.9 0.1 eq.20
  25.9 0.1 fusion.29
  26.0 0.1 reduce_window_sum.11
  26.1 0.2 select_reduce_fusion.2
  26.3 0.1 reshape.115
  26.3 0.1 reshape.116
  26.4 0.8 add_add_fusion
  27.2 0.0 collective-permute-done
  27.2 0.1 fusion.17
  27.4 0.8 fusion.19
  28.2 10.3 %collective-permute-start.2 = (bf16[16,4096]{1,0:T(8,128)(2,1)S(1)}, bf16[16,4096]{1,0:T(8,128)(2,1)S(1)}, u32[]{:S(2)}, u32[]{:S(2)}) collective-permute-start(bf16[16,4096]{1,0:T(8,128)(2,1)S(1)} %fusion.19), channel_id=1, source_target_pairs={{0,1},{1,0},{2,3},{3,2},{4,5},{5,4},{6,7},{7,6},{8,9},{9,8},{10,11... | collective-permute-start | bytes 393224 | tf_op jit(solution)/shard_map/ppermute | solution.py:11
  38.5 5.3 %collective-permute-done.2 = bf16[16,4096]{1,0:T(8,128)(2,1)S(1)} collective-permute-done((bf16[16,4096]{1,0:T(8,128)(2,1)S(1)}, bf16[16,4096]{1,0:T(8,128)(2,1)S(1)}, u32[]{:S(2)}, u32[]{:S(2)}) %collective-permute-start.2) | collective-permute-done | bytes 131104 | tf_op jit(solution)/shard_map/ppermute | solution.py:11
  43.8 1.1 fusion.22
  45.0 0.2 select_reduce_fusion.1
  45.2 0.1 convert_reduce_fusion
  45.3 0.5 convolution_convert_fusion.1
  45.8 1.2 reshape.117
  47.0 65.3 %all_to_all.15 = bf16[32,4,4096]{2,1,0:T(4,128)(2,1)S(1)} all-to-all(bf16[32,4,4096]{2,1,0:T(4,128)(2,1)} %reshape.117), channel_id=1, replica_groups=mesh['section'=2,'expert'=32,'y'=4,'zh'=2] {'expert'}, dimensions={0} | all-to-all | bytes 2097152 | tf_op jit(solution)/shard_map/all_to_all | solution.py:70
  112.3 2.1 stack.3
  114.4 50.4 %all_to_all.16 = bf16[4,1,32,4,4096]{4,3,2,1,0:T(4,128)(2,1)} all-to-all(bf16[4,1,32,4,4096]{4,3,2,1,0:T(4,128)(2,1)S(1)} %stack.3), channel_id=1, replica_groups=mesh['section'=2,'expert'=32,'y'=4,'zh'=2] {'y'}, dimensions={0} | all-to-all | bytes 8388608 | tf_op jit(solution)/shard_map/all_to_all | solution.py:72
  164.8 6.9 %reshape_reshape.3 = bf16[512,4096]{1,0:T(8,128)(2,1)} reshape(bf16[4,1,32,4,4096]{4,3,2,1,0:T(4,128)(2,1)} %all_to_all.16) | data formatting | bytes 8388608 | tf_op jit(solution)/shard_map/reshape;reshape | solution.py:74
  171.7 0.0 copy-done
  171.7 9.4 %convolution_convert_fusion = bf16[512,4096]{1,0:T(8,128)(2,1)} fusion(bf16[1,1,256,4096]{3,2,1,0:T(8,128)(2,1)S(1)} %copy-done, bf16[512,4096]{1,0:T(8,128)(2,1)} %reshape_reshape.3, bf16[1,1,4096,256]{3,2,1,0:T(8,128)(2,1)} %param.9), kind=kOutput, calls=%fused_computation | convolution fusion | flops 2150760448 | bytes 12582912 | tf_op jit(solution)/shard_map/dot_general | solution.py:78
  181.0 0.0 reduce-scatter.2.cloned.1.call-update
  181.1 54.6 %reduce-scatter.2.cloned.1.call-done = bf16[1,128,4096]{2,1,0:T(8,128)(2,1)} async-done(((bf16[4,128,4096]{2,1,0:T(8,128)(2,1)}), bf16[1,128,4096]{2,1,0:T(8,128)(2,1)}) %reduce-scatter.2.cloned.1.call-update) | async-done | bytes 1048592 | tf_op jit(solution)/shard_map/reduce_scatter | solution.py:79
  235.7 1.5 reshape.119
  237.2 62.2 %all_to_all.17 = bf16[32,4,4096]{2,1,0:T(4,128)(2,1)} all-to-all(bf16[32,4,4096]{2,1,0:T(4,128)(2,1)S(1)} %reshape.119), channel_id=1, replica_groups=mesh['section'=2,'expert'=32,'y'=4,'zh'=2] {'expert'}, dimensions={0} | all-to-all | bytes 2097152 | tf_op jit(solution)/shard_map/all_to_all | solution.py:82
  299.4 1.3 reshape.120
  300.7 0.5 fusion.39
  301.3 5.0 %collective-permute-start.3 = (bf16[16,4096]{1,0:T(8,128)(2,1)S(1)}, bf16[16,4096]{1,0:T(8,128)(2,1)S(1)}, u32[]{:S(2)}, u32[]{:S(2)}) collective-permute-start(bf16[16,4096]{1,0:T(8,128)(2,1)S(1)} %slice.15), channel_id=1, source_target_pairs={{0,1},{1,0},{2,3},{3,2},{4,5},{5,4},{6,7},{7,6},{8,9},{9,8},{10,11... | collective-permute-start | bytes 393224 | tf_op jit(solution)/shard_map/ppermute | solution.py:11
  306.3 16.9 %collective-permute-done.3 = bf16[16,4096]{1,0:T(8,128)(2,1)S(1)} collective-permute-done((bf16[16,4096]{1,0:T(8,128)(2,1)S(1)}, bf16[16,4096]{1,0:T(8,128)(2,1)S(1)}, u32[]{:S(2)}, u32[]{:S(2)}) %collective-permute-start.3) | collective-permute-done | bytes 131104 | tf_op jit(solution)/shard_map/ppermute | solution.py:11
  323.1 0.1 fusion.28
  323.2 2.4 collective-permute-start.4
  325.6 1.0 collective-permute-done.4
  326.6 0.7 copy.15
  (8 shorter events, 0.1 us)
Async XLA Ops:
  6.5 165.2 %copy-start = (bf16[1,1,256,4096]{3,2,1,0:T(8,128)(2,1)S(1)}, bf16[1,1,256,4096]{3,2,1,0:T(8,128)(2,1)}, u32[]{:S(2)}) copy-start(bf16[1,1,256,4096]{3,2,1,0:T(8,128)(2,1)} %param.10) | copy-start | bytes 6291460
  6.5 229.2 %reduce-scatter.2.cloned.1.call-start = ((), (), s32[]{:S(2)}) async-start(), calls=%async_computation.4 | async-start | bytes 5242880 | tf_op jit(solution)/shard_map/reduce_scatter | solution.py:79
  6.5 18.5 %collective-permute-start.1 = (s32[16,2]{0,1:T(2,128)}, s32[16,2]{0,1:T(2,128)S(1)}, u32[]{:S(2)}, u32[]{:S(2)}) collective-permute-start(s32[16,2]{0,1:T(2,128)} %bitcast.39), channel_id=1, source_target_pairs={{0,1},{1,0},{2,3},{3,2},{4,5},{5,4},{6,7},{7,6},{8,9},{9,8},{10,11... | collective-permute-start | bytes 392 | tf_op jit(solution)/shard_map/ppermute | solution.py:11
  22.1 5.1 %collective-permute-start = (bf16[1,16,4096]{2,1,0:T(8,128)(2,1)}, bf16[1,16,4096]{2,1,0:T(8,128)(2,1)S(1)}, u32[]{:S(2)}, u32[]{:S(2)}) collective-permute-start(bf16[1,16,4096]{2,1,0:T(8,128)(2,1)} %param.6), channel_id=1, source_target_pairs={{0,256},{256,0},{1,257},{257,1},{2,258},{258,2},{3,259},{259,3},{4... | collective-permute-start | bytes 393224 | tf_op jit(solution)/shard_map/ppermute | solution.py:11
  28.2 15.7 %collective-permute-start.2 = (bf16[16,4096]{1,0:T(8,128)(2,1)S(1)}, bf16[16,4096]{1,0:T(8,128)(2,1)S(1)}, u32[]{:S(2)}, u32[]{:S(2)}) collective-permute-start(bf16[16,4096]{1,0:T(8,128)(2,1)S(1)} %fusion.19), channel_id=1, source_target_pairs={{0,1},{1,0},{2,3},{3,2},{4,5},{5,4},{6,7},{7,6},{8,9},{9,8},{10,11... | collective-permute-start | bytes 393224 | tf_op jit(solution)/shard_map/ppermute | solution.py:11
  301.3 21.9 %collective-permute-start.3 = (bf16[16,4096]{1,0:T(8,128)(2,1)S(1)}, bf16[16,4096]{1,0:T(8,128)(2,1)S(1)}, u32[]{:S(2)}, u32[]{:S(2)}) collective-permute-start(bf16[16,4096]{1,0:T(8,128)(2,1)S(1)} %slice.15), channel_id=1, source_target_pairs={{0,1},{1,0},{2,3},{3,2},{4,5},{5,4},{6,7},{7,6},{8,9},{9,8},{10,11... | collective-permute-start | bytes 393224 | tf_op jit(solution)/shard_map/ppermute | solution.py:11
  323.2 3.4 %collective-permute-start.4 = (bf16[1,16,4096]{2,1,0:T(8,128)(2,1)S(1)}, bf16[1,16,4096]{2,1,0:T(8,128)(2,1)S(1)}, u32[]{:S(2)}, u32[]{:S(2)}) collective-permute-start(bf16[1,16,4096]{2,1,0:T(8,128)(2,1)S(1)} %fusion.28), channel_id=1, source_target_pairs={{0,256},{256,0},{1,257},{257,1},{2,258},{258,2},{3,259},{259,3},{4... | collective-permute-start | bytes 393224 | tf_op jit(solution)/shard_map/ppermute | solution.py:11
Sparse Core Ops, SparseCore 0:
  181.2 54.4 reduce-scatter.1
